TPU v7x, 512 devices: a whole 4x8x8 slice. The times are simulated.
512 devices in a mesh: dp: 32 (over y, z_lo, core), seq: 16 (over x, z_hi).
Axes of the slice: x: 4, y: 8, z: 8 (z_hi: 4, z_lo: 2; z = z_hi * 2 + z_lo), core: 2. Of those that a mesh axis runs over, the one named last changes fastest.
Arguments:
- query_rows: bfloat16 [32, 2048, 2048], P('dp', 'seq'), may hold values from -6 to 6
- key_rows: bfloat16 [32, 2048, 2048], P('dp', 'seq'), may hold values from -0.5 to 0.5
- value_rows: bfloat16 [32, 2048, 2048], P('dp', 'seq'), may hold values from -6 to 6
- doc_starts: int32 [32, 2048], P('dp', 'seq'), may hold values 0 or 1
- decay_rates: int32 [16], replicated, may hold values from 1 to 100
- out_gain: float32 [2048], replicated, may hold values from 0.1 to 1.9
- cotangent: bfloat16 [32, 2048, 2048], P('dp', 'seq'), may hold values from -6 to 6
Outputs:
- normed: bfloat16 [32, 2048, 2048], P('dp', 'seq')
- grad_query: bfloat16 [32, 2048, 2048], P('dp', 'seq')
- grad_key: bfloat16 [32, 2048, 2048], P('dp', 'seq')
- grad_value: bfloat16 [32, 2048, 2048], P('dp', 'seq')
- grad_gain: float32 [2048], P('dp')
All inputs are finite; a program needn't handle non-finite values. No bound on the sum of `doc_starts` on one device may be relied on, other than what follows from the above.
Results may differ from a plain program's by a relative error of at most 0.00085.
Values may be sent and summed in bfloat16 or wider, within the bound.
No kernel may reach another device: no remote copies, remote signals or barrier semaphores. Data moves between devices by JAX's collectives and lax.ppermute only.
A program may use at most 64 MiB of HBM per device.

v0:
```python
import math
import jax
import jax.numpy as jnp
from jax import lax
from jax.sharding import PartitionSpec as P

E = 128
highest = lax.Precision.HIGHEST
epsilon = 1e-05


def pack(factor, state):
    heads, width, _ = state.shape
    rows = jnp.broadcast_to(factor[:, None, None], (heads, 8, width))
    return jnp.concatenate([state, rows], axis=1)


def scan_exclusive(factor, state, reverse):
    count = lax.axis_size("seq")
    width = state.shape[1]
    run_factor, run_state = (factor, state)
    out_factor, out_state = (jnp.ones_like(factor), jnp.zeros_like(state))
    distance = 1
    while distance < count:
        if reverse:
            pairs = [(i, i - distance) for i in range(distance, count)]
        else:
            pairs = [(i, i + distance) for i in range(count - distance)]
        got = lax.ppermute(pack(run_factor, run_state), "seq", pairs)
        got_state, got_factor = (got[:, :width], got[:, width, 0])
        out_state = out_state + out_factor[:, None, None] * got_state
        out_factor = out_factor * got_factor
        if distance * 2 < count:
            run_state = run_state + run_factor[:, None, None] * got_state
            run_factor = run_factor * got_factor
        distance *= 2
    return out_state


def block_terms(log_decay, marks):
    length = marks.shape[0]
    counted = jnp.cumsum(marks, dtype=jnp.int32)
    places = jnp.arange(length, dtype=jnp.float32)
    offsets = places[:, None] - places[None, :]
    inside = (counted[:, None] == counted[None, :]) & (offsets >= 0.0)
    weights = jnp.where(
        inside[None], jnp.exp2(log_decay[:, None, None] * jnp.maximum(offsets, 0.0)[None]), 0.0
    )
    fresh = (counted == 0).astype(jnp.float32)
    entry = fresh[:, None] * jnp.exp2(log_decay[None, :] * (places[:, None] + 1.0))
    latest = counted[length - 1]
    tail = jnp.where(
        (counted == latest)[:, None],
        jnp.exp2(log_decay[None, :] * (length - 1.0 - places)[:, None]),
        0.0,
    )
    through = (latest == 0).astype(jnp.float32) * jnp.exp2(log_decay * length)
    return (weights, entry, tail, through)


def state_sum(key_block, value_block, tail):
    return jnp.einsum("jhe,jhf->hef", key_block * tail[:, :, None], value_block, precision=highest)


def out_sum(query_block, key_block, value_block, state_in, weights, entry):
    scores = jnp.einsum("ihe,jhe->hij", query_block, key_block, precision=highest) * weights
    inner = jnp.einsum("hij,jhe->ihe", scores, value_block, precision=highest)
    carried = jnp.einsum("ihe,hef->ihf", query_block, state_in, precision=highest)
    return inner + entry[:, :, None] * carried


def run_chain(through, terms, start, backward):

    def advance(accum, item):
        factor, term = item
        return (factor[:, None, None] * accum + term, accum)

    return lax.scan(advance, start, (through, terms), reverse=backward)


def ahead_state(factor, state):
    return scan_exclusive(factor, state, False)


def behind_grad(factor, state):
    return scan_exclusive(factor, state, True)


def forward_local(query_seq, key_seq, value_seq, marks, log_decay, link):
    length, heads, width = query_seq.shape
    block = math.gcd(length, 512)
    count = length // block
    query_blocks = query_seq.astype(jnp.float32).reshape(count, block, heads, width)
    key_blocks = key_seq.astype(jnp.float32).reshape(count, block, heads, width)
    value_blocks = value_seq.astype(jnp.float32).reshape(count, block, heads, width)
    weights, entry, tail, through = jax.vmap(block_terms, (None, 0))(
        log_decay, marks.reshape(count, block)
    )

    def states_of(key_part, value_part):
        return jax.vmap(state_sum)(key_part, value_part, tail)

    states, state_back = jax.vjp(states_of, key_blocks, value_blocks)
    empty = jnp.zeros((heads, width, width), jnp.float32)
    own_state = run_chain(through, states, empty, False)[0]
    own_factor = jnp.prod(through, axis=0)
    device_in = link(own_factor, own_state)
    block_in = run_chain(through, states, device_in, False)[1]

    def outs_of(query_part, key_part, value_part, state_part):
        return jax.vmap(out_sum)(query_part, key_part, value_part, state_part, weights, entry)

    outs, out_back = jax.vjp(outs_of, query_blocks, key_blocks, value_blocks, block_in)
    saved = (through, own_factor, state_back, out_back, block, count)
    return (outs.reshape(length, heads * width), saved)


def backward_local(grad_rows, saved, link, heads, width):
    through, own_factor, state_back, out_back, block, count = saved
    length = grad_rows.shape[0]
    grad_blocks = grad_rows.reshape(count, block, heads, width)
    grad_q_part, grad_k_part, grad_v_part, grad_state = out_back(grad_blocks)
    empty = jnp.zeros((heads, width, width), jnp.float32)
    own_grad = run_chain(through, grad_state, empty, True)[0]
    device_out = link(own_factor, own_grad)
    block_out = run_chain(through, grad_state, device_out, True)[1]
    extra_key, extra_value = state_back(block_out)
    flat = (length, heads * width)
    return (
        grad_q_part.reshape(flat),
        (grad_k_part + extra_key).reshape(flat),
        (grad_v_part + extra_value).reshape(flat),
    )


def normalize(mixed, out_gain, cotangent):

    def apply(attn, gain_vec):
        scale = lax.rsqrt(jnp.mean(attn * attn, axis=-1, keepdims=True) + epsilon)
        return attn * scale * gain_vec

    result, back = jax.vjp(apply, mixed, out_gain)
    grad_out, gain_part = back(cotangent.astype(jnp.float32))
    return (result.astype(jnp.bfloat16), grad_out, gain_part)


def per_device(query_rows, key_rows, value_rows, doc_starts, decay_rates, out_gain, cotangent):
    local_tokens = query_rows.shape[1]
    total = local_tokens * lax.axis_size("seq")
    log_decay = -decay_rates.astype(jnp.float32) / total
    heads = query_rows.shape[2] // E
    shaped = (local_tokens, heads, E)
    outs, saved = forward_local(
        query_rows[0].reshape(shaped),
        key_rows[0].reshape(shaped),
        value_rows[0].reshape(shaped),
        doc_starts[0],
        log_decay,
        ahead_state,
    )
    normed, grad_out, gain_part = normalize(outs[None], out_gain, cotangent)
    grads = backward_local(grad_out[0], saved, behind_grad, heads, E)
    grad_query = grads[0][None].astype(jnp.bfloat16)
    grad_key = grads[1][None].astype(jnp.bfloat16)
    grad_value = grads[2][None].astype(jnp.bfloat16)
    summed = lax.psum(gain_part, ("dp", "seq"))
    share = summed.shape[-1] // lax.axis_size("dp")
    grad_gain = lax.dynamic_slice_in_dim(summed, lax.axis_index("dp") * share, share)
    return (normed, grad_query, grad_key, grad_value, grad_gain)


def solution(mesh):
    return jax.shard_map(
        per_device,
        mesh=mesh,
        in_specs=(
            P("dp", "seq", None),
            P("dp", "seq", None),
            P("dp", "seq", None),
            P("dp", "seq"),
            P(),
            P(),
            P("dp", "seq", None),
        ),
        out_specs=(
            P("dp", "seq", None),
            P("dp", "seq", None),
            P("dp", "seq", None),
            P("dp", "seq", None),
            P("dp"),
        ),
        check_vma=False,
    )
```

profile of v0, /device:TPU:1, one launch (start us, length us, event | category | flops | bytes accessed | tf_op | source)
XLA Modules:
  0.0 497.9 jit_solution(8573685035798244976)
XLA Ops:
  7.5 6.7 %collective-permute-start = (f32[16,136,128]{2,1,0:T(8,128)}, f32[16,136,128]{2,1,0:T(8,128)S(1)}, u32[]{:S(2)}, u32[]{:S(2)}) collective-permute-start(f32[16,136,128]{2,1,0:T(8,128)} %pad_maximum_fusion.1), channel_id=1, source_target_pairs={{0,1},{1,2},{2,3},{3,4},{4,5},{5,6},{6,7},{7,8},{8,9},{9,10},{10,1... | collective-permute-start | bytes 3342344 | tf_op jit(solution)/shard_map/ppermute | solution.py:29
  14.3 22.9 %collective-permute-done = f32[16,136,128]{2,1,0:T(8,128)S(1)} collective-permute-done((f32[16,136,128]{2,1,0:T(8,128)}, f32[16,136,128]{2,1,0:T(8,128)S(1)}, u32[]{:S(2)}, u32[]{:S(2)}) %collective-permute-start) | collective-permute-done | bytes 1114144 | tf_op jit(solution)/shard_map/ppermute | solution.py:29
  37.7 35.3 %collective-permute-start.1 = (f32[16,136,128]{2,1,0:T(8,128)S(1)}, f32[16,136,128]{2,1,0:T(8,128)S(1)}, u32[]{:S(2)}, u32[]{:S(2)}) collective-permute-start(f32[16,136,128]{2,1,0:T(8,128)S(1)} %pad_maximum_fusion.2), channel_id=1, source_target_pairs={{0,2},{1,3},{2,4},{3,5},{4,6},{5,7},{6,8},{7,9},{8,10},{9,11},{10,... | collective-permute-start | bytes 3342344 | tf_op jit(solution)/shard_map/ppermute | solution.py:29
  73.0 29.5 %collective-permute-done.1 = f32[16,136,128]{2,1,0:T(8,128)S(1)} collective-permute-done((f32[16,136,128]{2,1,0:T(8,128)S(1)}, f32[16,136,128]{2,1,0:T(8,128)S(1)}, u32[]{:S(2)}, u32[]{:S(2)}) %collective-permute-start.1) | collective-permute-done | bytes 1114144 | tf_op jit(solution)/shard_map/ppermute | solution.py:29
  103.9 3.9 collective-permute-start.2
  107.8 12.4 %collective-permute-done.2 = f32[16,136,128]{2,1,0:T(8,128)S(1)} collective-permute-done((f32[16,136,128]{2,1,0:T(8,128)S(1)}, f32[16,136,128]{2,1,0:T(8,128)S(1)}, u32[]{:S(2)}, u32[]{:S(2)}) %collective-permute-start.2) | collective-permute-done | bytes 1114144 | tf_op jit(solution)/shard_map/ppermute | solution.py:29
  122.5 6.3 %collective-permute-start.3 = (f32[16,136,128]{2,1,0:T(8,128)}, f32[16,136,128]{2,1,0:T(8,128)}, u32[]{:S(2)}, u32[]{:S(2)}) collective-permute-start(f32[16,136,128]{2,1,0:T(8,128)} %pad_maximum_fusion.4), channel_id=1, source_target_pairs={{0,8},{1,9},{2,10},{3,11},{4,12},{5,13},{6,14},{7,15},{16,24},{17,... | collective-permute-start | bytes 3342344 | tf_op jit(solution)/shard_map/ppermute | solution.py:29
  131.1 20.1 %collective-permute-done.3 = f32[16,136,128]{2,1,0:T(8,128)} collective-permute-done((f32[16,136,128]{2,1,0:T(8,128)}, f32[16,136,128]{2,1,0:T(8,128)}, u32[]{:S(2)}, u32[]{:S(2)}) %collective-permute-start.3) | collective-permute-done | bytes 1114144 | tf_op jit(solution)/shard_map/ppermute | solution.py:29
  151.2 1.6 fusion.13
  152.8 2.0 multiply_reduce_fusion
  154.8 1.6 copy.45
  156.9 1.6 add_add_fusion
  158.6 1.5 copy.48
  162.7 80.2 %collective-permute-done.4 = f32[16,136,128]{2,1,0:T(8,128)S(1)} collective-permute-done((f32[16,136,128]{2,1,0:T(8,128)S(1)}, f32[16,136,128]{2,1,0:T(8,128)S(1)}, u32[]{:S(2)}, u32[]{:S(2)}) %collective-permute-start.4) | collective-permute-done | bytes 1114144 | tf_op jit(solution)/shard_map/ppermute | solution.py:29
  244.8 74.5 %collective-permute-done.5 = f32[16,136,128]{2,1,0:T(8,128)S(1)} collective-permute-done((f32[16,136,128]{2,1,0:T(8,128)S(1)}, f32[16,136,128]{2,1,0:T(8,128)S(1)}, u32[]{:S(2)}, u32[]{:S(2)}) %collective-permute-start.5) | collective-permute-done | bytes 1114144 | tf_op jit(solution)/shard_map/ppermute | solution.py:29
  322.9 43.6 %collective-permute-done.6 = f32[16,136,128]{2,1,0:T(8,128)} collective-permute-done((f32[16,136,128]{2,1,0:T(8,128)}, f32[16,136,128]{2,1,0:T(8,128)}, u32[]{:S(2)}, u32[]{:S(2)}) %collective-permute-start.6) | collective-permute-done | bytes 1114144 | tf_op jit(solution)/shard_map/ppermute | solution.py:29
  366.6 1.4 multiply_add_fusion
  370.2 1.5 collective-permute-start.7
  374.1 2.0 fusion.5
  376.1 2.0 copy.57
  378.2 108.3 %psum.7 = f32[2048]{0:T(1024)S(1)} all-reduce(f32[2048]{0:T(1024)S(1)} %get-tuple-element.64), channel_id=1, replica_groups=mesh['dp'=32,'seq'=16] {'dp','seq'}, use_global_device_ids=true, to_apply=%region_4.5 | all-reduce | flops 2048 | bytes 16384 | tf_op jit(solution)/shard_map/psum | solution.py:166
  487.0 1.8 convolution_bitcast_fusion.2
  490.4 1.9 fusion.12
  492.4 2.3 fusion.6
  (96 shorter events, 31.0 us)
Async XLA Ops:
  0.6 4.1 copy-start.16
  0.6 4.2 copy-start.19
  7.5 29.7 %collective-permute-start = (f32[16,136,128]{2,1,0:T(8,128)}, f32[16,136,128]{2,1,0:T(8,128)S(1)}, u32[]{:S(2)}, u32[]{:S(2)}) collective-permute-start(f32[16,136,128]{2,1,0:T(8,128)} %pad_maximum_fusion.1), channel_id=1, source_target_pairs={{0,1},{1,2},{2,3},{3,4},{4,5},{5,6},{6,7},{7,8},{8,9},{9,10},{10,1... | collective-permute-start | bytes 3342344 | tf_op jit(solution)/shard_map/ppermute | solution.py:29
  37.1 65.6 %copy-start.7 = (f32[16,136,128]{2,1,0:T(8,128)}, f32[16,136,128]{2,1,0:T(8,128)S(1)}, u32[]{:S(2)}) copy-start(f32[16,136,128]{2,1,0:T(8,128)S(1)} %collective-permute-done) | copy-start | bytes 3342340
  37.7 64.8 %collective-permute-start.1 = (f32[16,136,128]{2,1,0:T(8,128)S(1)}, f32[16,136,128]{2,1,0:T(8,128)S(1)}, u32[]{:S(2)}, u32[]{:S(2)}) collective-permute-start(f32[16,136,128]{2,1,0:T(8,128)S(1)} %pad_maximum_fusion.2), channel_id=1, source_target_pairs={{0,2},{1,3},{2,4},{3,5},{4,6},{5,7},{6,8},{7,9},{8,10},{9,11},{10,... | collective-permute-start | bytes 3342344 | tf_op jit(solution)/shard_map/ppermute | solution.py:29
  103.9 16.3 %collective-permute-start.2 = (f32[16,136,128]{2,1,0:T(8,128)S(1)}, f32[16,136,128]{2,1,0:T(8,128)S(1)}, u32[]{:S(2)}, u32[]{:S(2)}) collective-permute-start(f32[16,136,128]{2,1,0:T(8,128)S(1)} %pad_maximum_fusion.3), channel_id=1, source_target_pairs={{0,4},{1,5},{2,6},{3,7},{4,8},{5,9},{6,10},{7,11},{8,12},{9,13},{1... | collective-permute-start | bytes 3342344 | tf_op jit(solution)/shard_map/ppermute | solution.py:29
  121.5 7.4 %copy-start.17 = (bf16[1,128,2048]{2,1,0:T(8,128)(2,1)S(1)}, bf16[1,128,2048]{2,1,0:T(8,128)(2,1)}, u32[]{:S(2)}) copy-start(bf16[1,128,2048]{2,1,0:T(8,128)(2,1)} %param.7) | copy-start | bytes 1572868
  122.5 28.6 %collective-permute-start.3 = (f32[16,136,128]{2,1,0:T(8,128)}, f32[16,136,128]{2,1,0:T(8,128)}, u32[]{:S(2)}, u32[]{:S(2)}) collective-permute-start(f32[16,136,128]{2,1,0:T(8,128)} %pad_maximum_fusion.4), channel_id=1, source_target_pairs={{0,8},{1,9},{2,10},{3,11},{4,12},{5,13},{6,14},{7,15},{16,24},{17,... | collective-permute-start | bytes 3342344 | tf_op jit(solution)/shard_map/ppermute | solution.py:29
  129.2 30.9 %copy-start.2 = (bf16[1,128,2048]{1,2,0:T(8,128)(2,1)}, bf16[1,128,2048]{1,2,0:T(8,128)(2,1)S(1)}, u32[]{:S(2)}) copy-start(bf16[1,128,2048]{1,2,0:T(8,128)(2,1)S(1)} %copy.64) | copy-start | bytes 1572868
  129.3 21.9 %copy-start.14 = (f32[16,136,128]{2,1,0:T(8,128)S(1)}, f32[16,136,128]{2,1,0:T(8,128)}, u32[]{:S(2)}) copy-start(f32[16,136,128]{2,1,0:T(8,128)} %copy-done.13) | copy-start | bytes 3342340
  129.9 21.3 %copy-start.8 = (f32[16,136,128]{2,1,0:T(8,128)S(1)}, f32[16,136,128]{2,1,0:T(8,128)}, u32[]{:S(2)}) copy-start(f32[16,136,128]{2,1,0:T(8,128)} %copy-done.7) | copy-start | bytes 3342340
  129.9 21.3 %copy-start.12 = (f32[16,136,128]{2,1,0:T(8,128)S(1)}, f32[16,136,128]{2,1,0:T(8,128)}, u32[]{:S(2)}) copy-start(f32[16,136,128]{2,1,0:T(8,128)} %copy-done.11) | copy-start | bytes 3342340
  152.8 2.0 copy-start
  154.8 1.6 copy-start.15
  154.8 1.6 copy-start.18
  161.4 81.5 %collective-permute-start.4 = (f32[16,136,128]{2,1,0:T(8,128)S(1)}, f32[16,136,128]{2,1,0:T(8,128)S(1)}, u32[]{:S(2)}, u32[]{:S(2)}) collective-permute-start(f32[16,136,128]{2,1,0:T(8,128)S(1)} %pad_maximum_fusion), channel_id=1, source_target_pairs={{1,0},{2,1},{3,2},{4,3},{5,4},{6,5},{7,6},{8,7},{9,8},{10,9},{11,1... | collective-permute-start | bytes 3342344 | tf_op jit(solution)/shard_map/ppermute | solution.py:29
  242.9 76.5 %copy-start.5 = (f32[16,136,128]{2,1,0:T(8,128)}, f32[16,136,128]{2,1,0:T(8,128)S(1)}, u32[]{:S(2)}) copy-start(f32[16,136,128]{2,1,0:T(8,128)S(1)} %collective-permute-done.4) | copy-start | bytes 3342340
  243.5 75.8 %collective-permute-start.5 = (f32[16,136,128]{2,1,0:T(8,128)S(1)}, f32[16,136,128]{2,1,0:T(8,128)S(1)}, u32[]{:S(2)}, u32[]{:S(2)}) collective-permute-start(f32[16,136,128]{2,1,0:T(8,128)S(1)} %pad_maximum_fusion.5), channel_id=1, source_target_pairs={{2,0},{3,1},{4,2},{5,3},{6,4},{7,5},{8,6},{9,7},{10,8},{11,9},{12,... | collective-permute-start | bytes 3342344 | tf_op jit(solution)/shard_map/ppermute | solution.py:29
  321.7 44.9 %collective-permute-start.6 = (f32[16,136,128]{2,1,0:T(8,128)}, f32[16,136,128]{2,1,0:T(8,128)}, u32[]{:S(2)}, u32[]{:S(2)}) collective-permute-start(f32[16,136,128]{2,1,0:T(8,128)} %pad_maximum_fusion.6), channel_id=1, source_target_pairs={{4,0},{5,1},{6,2},{7,3},{8,4},{9,5},{10,6},{11,7},{12,8},{13,9},{1... | collective-permute-start | bytes 3342344 | tf_op jit(solution)/shard_map/ppermute | solution.py:29
  370.2 119.8 %collective-permute-start.7 = (f32[16,136,128]{2,1,0:T(8,128)}, f32[16,136,128]{2,1,0:T(8,128)}, u32[]{:S(2)}, u32[]{:S(2)}) collective-permute-start(f32[16,136,128]{2,1,0:T(8,128)} %pad_maximum_fusion.7), channel_id=1, source_target_pairs={{8,0},{9,1},{10,2},{11,3},{12,4},{13,5},{14,6},{15,7},{24,16},{25,... | collective-permute-start | bytes 3342344 | tf_op jit(solution)/shard_map/ppermute | solution.py:29
  372.9 1.2 copy-start.1
  487.0 1.8 copy-start.4
  488.8 1.2 copy-start.6
  488.9 1.6 copy-start.10
  (4 other events, 4.2 us)
where the time goes:
time: 499 us; the launch traced here: 498 us
  waiting for transfers between devices  283 us (57%)
  blocking collectives  108 us (22%)
  starting transfers between devices  57.6 us (12%)
  matrix products  17.2 us (3%)
  other arithmetic  16.4 us (3%)
  local copies, waits for them, and re-layouts  13.5 us (3%)
    ppermute x8, waiting for transfers between devices, scan_exclusive(): got = lax.ppermute(pack(run_factor, run_state), 'seq', pairs)  283 us
    psum x1, blocking collectives, per_device(): summed = lax.psum(gain_part, ('dp', 'seq'))  108 us
    ppermute x8, starting transfers between devices, scan_exclusive(): got = lax.ppermute(pack(run_factor, run_state), 'seq', pairs)  57.6 us
  transfers between devices with their start and end apart: 8, of which 7 were waited for; matrix products, arithmetic and copies ran while one was open for 2% of the time, Pallas kernels for 0%

commit v1 on v0

--- a/solution.py
+++ b/solution.py
@@ -163,7 +163,7 @@
     grad_query = grads[0][None].astype(jnp.bfloat16)
     grad_key = grads[1][None].astype(jnp.bfloat16)
     grad_value = grads[2][None].astype(jnp.bfloat16)
-    summed = lax.psum(gain_part, ("dp", "seq"))
+    summed = jnp.sum(lax.all_gather(gain_part, ("dp", "seq")), axis=0)
     share = summed.shape[-1] // lax.axis_size("dp")
     grad_gain = lax.dynamic_slice_in_dim(summed, lax.axis_index("dp") * share, share)
     return (normed, grad_query, grad_key, grad_value, grad_gain)

time: 499 us -> 1670 us (3.35)
  waiting for transfers between devices: 283 us -> 1530 us
  blocking collectives: 108 us -> 0 us
    all_gather x0 -> x1, waiting for transfers between devices: none -> 1220 us  [per_device(): summed = jnp.sum(lax.all_gather(gain_part, ('dp', 'seq')), axis=0)]
    psum x1 -> x0, blocking collectives: 108 us -> none  [per_device(): summed = lax.psum(gain_part, ('dp', 'seq'))]
    ppermute x8, waiting for transfers between devices: 283 us -> 306 us  [scan_exclusive(): got = lax.ppermute(pack(run_factor, run_state), 'seq', pairs)]
  transfers between devices with their start and end apart: 8 -> 9, of which waited for: 7 -> 9; matrix products, arithmetic and copies ran while one was open for 2% -> 2% of each run, Pallas kernels for 0% -> 0%
where the time goes in v1:
time: 1670 us; the launch traced here: 1660 us
  waiting for transfers between devices  1530 us (92%)
  starting transfers between devices  57.6 us (3%)
  other arithmetic  19.5 us (1%)
  local copies, waits for them, and re-layouts  18.6 us (1%)
  matrix products  18 us (1%)
    all_gather x1, waiting for transfers between devices, per_device(): summed = jnp.sum(lax.all_gather(gain_part, ('dp', 'seq')), axis=0)  1220 us
    ppermute x8, waiting for transfers between devices, scan_exclusive(): got = lax.ppermute(pack(run_factor, run_state), 'seq', pairs)  306 us
    ppermute x8, starting transfers between devices, scan_exclusive(): got = lax.ppermute(pack(run_factor, run_state), 'seq', pairs)  57.5 us
  transfers between devices with their start and end apart: 9, of which 9 were waited for; matrix products, arithmetic and copies ran while one was open for 2% of the time, Pallas kernels for 0%

profile of v1, /device:TPU:1, one launch (start us, length us, event | category | flops | bytes accessed | tf_op | source)
XLA Modules:
  0.0 1658.9 jit_solution(12745137814062521020)
XLA Ops:
  14.0 6.7 collective-permute-start
  20.8 22.9 %collective-permute-done = f32[16,136,128]{2,1,0:T(8,128)S(1)} collective-permute-done((f32[16,136,128]{2,1,0:T(8,128)}, f32[16,136,128]{2,1,0:T(8,128)S(1)}, u32[]{:S(2)}, u32[]{:S(2)}) %collective-permute-start) | collective-permute-done | bytes 1114144 | tf_op jit(solution)/shard_map/ppermute | solution.py:29
  44.2 35.3 %collective-permute-start.1 = (f32[16,136,128]{2,1,0:T(8,128)S(1)}, f32[16,136,128]{2,1,0:T(8,128)S(1)}, u32[]{:S(2)}, u32[]{:S(2)}) collective-permute-start(f32[16,136,128]{2,1,0:T(8,128)S(1)} %pad_maximum_fusion.2), channel_id=1, source_target_pairs={{0,2},{1,3},{2,4},{3,5},{4,6},{5,7},{6,8},{7,9},{8,10},{9,11},{10,... | collective-permute-start | bytes 3342344 | tf_op jit(solution)/shard_map/ppermute | solution.py:29
  79.6 29.5 %collective-permute-done.1 = f32[16,136,128]{2,1,0:T(8,128)S(1)} collective-permute-done((f32[16,136,128]{2,1,0:T(8,128)S(1)}, f32[16,136,128]{2,1,0:T(8,128)S(1)}, u32[]{:S(2)}, u32[]{:S(2)}) %collective-permute-start.1) | collective-permute-done | bytes 1114144 | tf_op jit(solution)/shard_map/ppermute | solution.py:29
  110.3 3.9 collective-permute-start.2
  114.2 12.4 collective-permute-done.2
  128.9 6.3 collective-permute-start.3
  137.4 20.1 %collective-permute-done.3 = f32[16,136,128]{2,1,0:T(8,128)} collective-permute-done((f32[16,136,128]{2,1,0:T(8,128)}, f32[16,136,128]{2,1,0:T(8,128)}, u32[]{:S(2)}, u32[]{:S(2)}) %collective-permute-start.3) | collective-permute-done | bytes 1114144 | tf_op jit(solution)/shard_map/ppermute | solution.py:29
  159.2 2.0 multiply_reduce_fusion
  163.9 1.6 add_add_fusion
  169.7 80.6 %collective-permute-done.4 = f32[16,136,128]{2,1,0:T(8,128)S(1)} collective-permute-done((f32[16,136,128]{2,1,0:T(8,128)S(1)}, f32[16,136,128]{2,1,0:T(8,128)S(1)}, u32[]{:S(2)}, u32[]{:S(2)}) %collective-permute-start.4) | collective-permute-done | bytes 1114144 | tf_op jit(solution)/shard_map/ppermute | solution.py:29
  252.1 75.0 %collective-permute-done.5 = f32[16,136,128]{2,1,0:T(8,128)S(1)} collective-permute-done((f32[16,136,128]{2,1,0:T(8,128)S(1)}, f32[16,136,128]{2,1,0:T(8,128)S(1)}, u32[]{:S(2)}, u32[]{:S(2)}) %collective-permute-start.5) | collective-permute-done | bytes 1114144 | tf_op jit(solution)/shard_map/ppermute | solution.py:29
  330.6 43.3 %collective-permute-done.6 = f32[16,136,128]{2,1,0:T(8,128)} collective-permute-done((f32[16,136,128]{2,1,0:T(8,128)}, f32[16,136,128]{2,1,0:T(8,128)}, u32[]{:S(2)}, u32[]{:S(2)}) %collective-permute-start.6) | collective-permute-done | bytes 1114144 | tf_op jit(solution)/shard_map/ppermute | solution.py:29
  381.5 2.0 fusion.5
  383.5 2.0 copy.105
  385.5 1.8 convolution_bitcast_fusion.2
  388.5 21.9 %collective-permute-done.7 = f32[16,136,128]{2,1,0:T(8,128)} collective-permute-done((f32[16,136,128]{2,1,0:T(8,128)}, f32[16,136,128]{2,1,0:T(8,128)}, u32[]{:S(2)}, u32[]{:S(2)}) %collective-permute-start.7) | collective-permute-done | bytes 1114144 | tf_op jit(solution)/shard_map/ppermute | solution.py:29
  410.4 1.9 fusion.12
  412.3 2.0 fusion.7
  414.4 2.0 copy.106
  416.4 2.3 fusion.6
  419.7 1224.4 %all-gather.3.cloned.1.call-done = f32[1048576]{0:T(1024)} async-done(((f32[2048]{0:T(1024)}), f32[1048576]{0:T(1024)}) %all-gather.3.cloned.1.call-update) | async-done | bytes 4194320 | tf_op jit(solution)/shard_map/all_gather | solution.py:166
  1644.1 4.9 reshape.553
  1649.0 2.4 reduce_sum.41
  (100 shorter events, 36.3 us)
Async XLA Ops:
  7.2 3.5 copy-start.16
  7.2 4.3 copy-start.19
  7.2 1636.9 %all-gather.3.cloned.1.call-start = ((), (), s32[]{:S(2)}) async-start(), calls=%async_computation | async-start | bytes 4202496 | tf_op jit(solution)/shard_map/all_gather | solution.py:166
  14.0 29.7 %collective-permute-start = (f32[16,136,128]{2,1,0:T(8,128)}, f32[16,136,128]{2,1,0:T(8,128)S(1)}, u32[]{:S(2)}, u32[]{:S(2)}) collective-permute-start(f32[16,136,128]{2,1,0:T(8,128)} %pad_maximum_fusion.1), channel_id=1, source_target_pairs={{0,1},{1,2},{2,3},{3,4},{4,5},{5,6},{6,7},{7,8},{8,9},{9,10},{10,1... | collective-permute-start | bytes 3342344 | tf_op jit(solution)/shard_map/ppermute | solution.py:29
  43.7 65.4 %copy-start.7 = (f32[16,136,128]{2,1,0:T(8,128)}, f32[16,136,128]{2,1,0:T(8,128)S(1)}, u32[]{:S(2)}) copy-start(f32[16,136,128]{2,1,0:T(8,128)S(1)} %collective-permute-done) | copy-start | bytes 3342340
  44.2 64.9 %collective-permute-start.1 = (f32[16,136,128]{2,1,0:T(8,128)S(1)}, f32[16,136,128]{2,1,0:T(8,128)S(1)}, u32[]{:S(2)}, u32[]{:S(2)}) collective-permute-start(f32[16,136,128]{2,1,0:T(8,128)S(1)} %pad_maximum_fusion.2), channel_id=1, source_target_pairs={{0,2},{1,3},{2,4},{3,5},{4,6},{5,7},{6,8},{7,9},{8,10},{9,11},{10,... | collective-permute-start | bytes 3342344 | tf_op jit(solution)/shard_map/ppermute | solution.py:29
  110.3 16.3 collective-permute-start.2
  127.8 7.4 copy-start.17
  128.9 28.6 %collective-permute-start.3 = (f32[16,136,128]{2,1,0:T(8,128)}, f32[16,136,128]{2,1,0:T(8,128)}, u32[]{:S(2)}, u32[]{:S(2)}) collective-permute-start(f32[16,136,128]{2,1,0:T(8,128)} %pad_maximum_fusion.4), channel_id=1, source_target_pairs={{0,8},{1,9},{2,10},{3,11},{4,12},{5,13},{6,14},{7,15},{16,24},{17,... | collective-permute-start | bytes 3342344 | tf_op jit(solution)/shard_map/ppermute | solution.py:29
  135.5 31.6 %copy-start.2 = (bf16[1,128,2048]{1,2,0:T(8,128)(2,1)}, bf16[1,128,2048]{1,2,0:T(8,128)(2,1)S(1)}, u32[]{:S(2)}) copy-start(bf16[1,128,2048]{1,2,0:T(8,128)(2,1)S(1)} %copy.112) | copy-start | bytes 1572868
  135.6 21.9 %copy-start.14 = (f32[16,136,128]{2,1,0:T(8,128)S(1)}, f32[16,136,128]{2,1,0:T(8,128)}, u32[]{:S(2)}) copy-start(f32[16,136,128]{2,1,0:T(8,128)} %copy-done.13) | copy-start | bytes 3342340
  136.2 21.4 %copy-start.8 = (f32[16,136,128]{2,1,0:T(8,128)S(1)}, f32[16,136,128]{2,1,0:T(8,128)}, u32[]{:S(2)}) copy-start(f32[16,136,128]{2,1,0:T(8,128)} %copy-done.7) | copy-start | bytes 3342340
  136.2 21.4 %copy-start.12 = (f32[16,136,128]{2,1,0:T(8,128)S(1)}, f32[16,136,128]{2,1,0:T(8,128)}, u32[]{:S(2)}) copy-start(f32[16,136,128]{2,1,0:T(8,128)} %copy-done.11) | copy-start | bytes 3342340
  159.2 2.1 copy-start
  161.2 1.6 copy-start.15
  161.2 1.6 copy-start.18
  168.4 81.9 %collective-permute-start.4 = (f32[16,136,128]{2,1,0:T(8,128)S(1)}, f32[16,136,128]{2,1,0:T(8,128)S(1)}, u32[]{:S(2)}, u32[]{:S(2)}) collective-permute-start(f32[16,136,128]{2,1,0:T(8,128)S(1)} %pad_maximum_fusion), channel_id=1, source_target_pairs={{1,0},{2,1},{3,2},{4,3},{5,4},{6,5},{7,6},{8,7},{9,8},{10,9},{11,1... | collective-permute-start | bytes 3342344 | tf_op jit(solution)/shard_map/ppermute | solution.py:29
  250.3 76.8 %copy-start.5 = (f32[16,136,128]{2,1,0:T(8,128)}, f32[16,136,128]{2,1,0:T(8,128)S(1)}, u32[]{:S(2)}) copy-start(f32[16,136,128]{2,1,0:T(8,128)S(1)} %collective-permute-done.4) | copy-start | bytes 3342340
  250.8 76.3 %collective-permute-start.5 = (f32[16,136,128]{2,1,0:T(8,128)S(1)}, f32[16,136,128]{2,1,0:T(8,128)S(1)}, u32[]{:S(2)}, u32[]{:S(2)}) collective-permute-start(f32[16,136,128]{2,1,0:T(8,128)S(1)} %pad_maximum_fusion.5), channel_id=1, source_target_pairs={{2,0},{3,1},{4,2},{5,3},{6,4},{7,5},{8,6},{9,7},{10,8},{11,9},{12,... | collective-permute-start | bytes 3342344 | tf_op jit(solution)/shard_map/ppermute | solution.py:29
  329.3 44.6 %collective-permute-start.6 = (f32[16,136,128]{2,1,0:T(8,128)}, f32[16,136,128]{2,1,0:T(8,128)}, u32[]{:S(2)}, u32[]{:S(2)}) collective-permute-start(f32[16,136,128]{2,1,0:T(8,128)} %pad_maximum_fusion.6), channel_id=1, source_target_pairs={{4,0},{5,1},{6,2},{7,3},{8,4},{9,5},{10,6},{11,7},{12,8},{13,9},{1... | collective-permute-start | bytes 3342344 | tf_op jit(solution)/shard_map/ppermute | solution.py:29
  377.6 32.8 %collective-permute-start.7 = (f32[16,136,128]{2,1,0:T(8,128)}, f32[16,136,128]{2,1,0:T(8,128)}, u32[]{:S(2)}, u32[]{:S(2)}) collective-permute-start(f32[16,136,128]{2,1,0:T(8,128)} %pad_maximum_fusion.7), channel_id=1, source_target_pairs={{8,0},{9,1},{10,2},{11,3},{12,4},{13,5},{14,6},{15,7},{24,16},{25,... | collective-permute-start | bytes 3342344 | tf_op jit(solution)/shard_map/ppermute | solution.py:29
  385.5 1.8 copy-start.4
  387.3 23.1 %copy-start.6 = (f32[16,136,128]{2,1,0:T(8,128)S(1)}, f32[16,136,128]{2,1,0:T(8,128)}, u32[]{:S(2)}) copy-start(f32[16,136,128]{2,1,0:T(8,128)} %copy-done.5) | copy-start | bytes 3342340
  387.4 23.0 %copy-start.10 = (f32[16,136,128]{2,1,0:T(8,128)S(1)}, f32[16,136,128]{2,1,0:T(8,128)}, u32[]{:S(2)}) copy-start(f32[16,136,128]{2,1,0:T(8,128)} %copy-done.9) | copy-start | bytes 3342340
  (5 other events, 5.5 us)
Sparse Core Ops, SparseCore 0:
  164.0 1480.0 all-gather.2
